TPU v7x, 256 devices: a whole 4x4x8 slice. The times are simulated.
256 devices in a mesh: grp: 4 (over x), tok: 8 (over z), mdl: 8 (over y, core).
Axes of the slice: x: 4, y: 4, z: 8, core: 2. Of those that a mesh axis runs over, the one named last changes fastest.
Arguments:
- hidden_in: bfloat16 [4, 1024, 5120], P('grp', 'tok', 'mdl'), may hold values from -8 to 8
- seg_ids: int32 [4, 1024], replicated, may hold values from 0 to 3, never falling along the last dimension, each value on 1 to 768 neighbouring positions
- request_prefix: int32 [4, 4], replicated, may hold values from 0 to 1
- page_table: int32 [32], replicated, may hold values from 0 to 31, each once
- prefix_cache: bfloat16 [32, 256, 8, 256], P(('grp', 'mdl'), None, 'tok'), may hold values from -200 to 200
- attn_gain: float32 [5120], P('mdl'), may hold values from 0.1 to 1.9
- w_query: bfloat16 [5120, 5120], P('mdl', 'tok'), may hold values from -0.078125 to 0.078125
- w_key: bfloat16 [5120, 1024], P('mdl', 'tok'), may hold values from -0.25 to 0.25
- w_value: bfloat16 [5120, 1024], P('mdl', 'tok'), may hold values from -0.078125 to 0.078125
- w_out: bfloat16 [5120, 5120], P('tok', 'mdl'), may hold values from -0.078125 to 0.078125
- ffn_gain: float32 [5120], P('mdl'), may hold values from 0.1 to 1.9
- w_gate: bfloat16 [5120, 14336], P('mdl', 'tok'), may hold values from -0.078125 to 0.078125
- w_up: bfloat16 [5120, 14336], P('mdl', 'tok'), may hold values from -0.078125 to 0.078125
- w_down: bfloat16 [14336, 5120], P('tok', 'mdl'), may hold values from -0.046875 to 0.046875
- final_gain: float32 [5120], replicated, may hold values from 0.1 to 1.9
- lm_head: bfloat16 [76800, 5120], P(('grp', 'tok', 'mdl')), may hold values from -0.25 to 0.25
Outputs:
- hidden_out: bfloat16 [4, 1024, 5120], P('grp', 'tok', 'mdl')
- new_kv: bfloat16 [4, 1024, 8, 256], P('grp', 'mdl', 'tok')
- req_norm: float32 [4, 4], P('grp')
- max_logit: float32 [4, 4], replicated
- logits: float32 [16, 76800], P(None, ('grp', 'tok', 'mdl'))
Inputs may be any that keep to these rules, and one draw needn't show every extreme that they name: `seg_ids`: requests of a group are contiguous, in order, and none is empty. `page_table`: each physical slot holds exactly one logical page.
All inputs are finite; a program needn't handle non-finite values.
Results may differ from a plain program's by a relative error of at most 0.024.
Values may be sent and summed in bfloat16 or wider, within the bound.
No kernel may reach another device: no remote copies, remote signals or barrier semaphores. Data moves between devices by JAX's collectives and lax.ppermute only.
A program may use at most 128 MiB of HBM per device.

v0:
```python
import jax
import jax.numpy as jnp
from jax import lax
from jax.sharding import PartitionSpec as P

PREFIX = 4096
PAGE = 256
EPS = 1e-06
THETA = 1000000.0
NEG = -1e30


def rotate(tensor, positions):
    half_dim = tensor.shape[-1] // 2
    frequency = THETA ** (-(jnp.arange(half_dim, dtype=jnp.float32) * 2.0 / tensor.shape[-1]))
    angles = positions.astype(jnp.float32)[:, None] * frequency[None, :]
    cosine = jnp.cos(angles)[:, None, :]
    sine_part = jnp.sin(angles)[:, None, :]
    first_part = tensor[..., :half_dim]
    second = tensor[..., half_dim:]
    return jnp.concatenate(
        [first_part * cosine - second * sine_part, second * cosine + first_part * sine_part], -1
    )


def on_device(
    hidden_in,
    seg_ids,
    request_prefix,
    page_table,
    prefix_cache,
    attn_gain,
    w_query,
    w_key,
    w_value,
    w_out,
    ffn_gain,
    w_gate,
    w_up,
    w_down,
    final_gain,
    lm_head,
):
    groups_total = seg_ids.shape[0]
    seq_len = seg_ids.shape[1]
    req_count = request_prefix.shape[1]
    tok_rows = hidden_in.shape[1]
    feat_dev = hidden_in.shape[2]
    model_width = feat_dev * lax.axis_size("mdl")
    head_dim = prefix_cache.shape[3] // 2
    kv_dev = prefix_cache.shape[2]
    heads_dev = w_query.shape[1] // head_dim
    group_size = heads_dev // kv_dev
    page_len = prefix_cache.shape[1]
    slot_total = page_table.shape[0]
    rows_mdl = seq_len // lax.axis_size("mdl")
    group_idx = lax.axis_index("grp")
    tok_idx = lax.axis_index("tok")
    mdl_idx = lax.axis_index("mdl")
    score_scale = head_dim ** (-0.5)
    tokens = hidden_in[0].astype(jnp.float32)
    squares = lax.psum(jnp.sum(tokens * tokens, -1), "mdl")
    normed = (tokens * lax.rsqrt(squares[:, None] / model_width + EPS) * attn_gain).astype(
        jnp.bfloat16
    )
    w_joined = jnp.concatenate([w_query, w_key, w_value], 1)
    partial_qkv = jnp.dot(
        lax.all_gather(normed, "tok", axis=0, tiled=True),
        w_joined,
        preferred_element_type=jnp.float32,
    )
    qkv_rows = lax.psum_scatter(partial_qkv, "mdl", scatter_dimension=0, tiled=True)
    q_cols = heads_dev * head_dim
    kv_cols = kv_dev * head_dim
    queries = qkv_rows[:, :q_cols].reshape(rows_mdl, heads_dev, head_dim)
    key_rows = qkv_rows[:, q_cols : q_cols + kv_cols].reshape(rows_mdl, kv_dev, head_dim)
    value_rows = qkv_rows[:, q_cols + kv_cols :].reshape(rows_mdl, kv_dev, head_dim)
    seg_row = lax.dynamic_index_in_dim(seg_ids, group_idx, 0, keepdims=False)
    prefix_row = lax.dynamic_index_in_dim(request_prefix, group_idx, 0, keepdims=False)
    requests = jnp.arange(req_count, dtype=jnp.int32)
    member = seg_row[:, None] == requests[None, :]
    counts = jnp.sum(member.astype(jnp.int32), 0)
    offsets = jnp.cumsum(counts) - counts
    row_start = mdl_idx * rows_mdl
    my_rows = row_start + jnp.arange(rows_mdl, dtype=jnp.int32)
    my_seg = lax.dynamic_slice_in_dim(seg_row, row_start, rows_mdl)
    my_member = my_seg[:, None] == requests[None, :]
    positions = PREFIX + my_rows - jnp.sum(jnp.where(my_member, offsets[None, :], 0), 1)
    my_prefix = jnp.sum(jnp.where(my_member, prefix_row[None, :], 0), 1)
    q_rot = (
        rotate(queries, positions)
        .astype(jnp.bfloat16)
        .reshape(rows_mdl, kv_dev, group_size, head_dim)
    )
    k_rot = rotate(key_rows, positions).astype(jnp.bfloat16)
    appended = jnp.concatenate([k_rot, value_rows.astype(jnp.bfloat16)], -1)
    suffix = lax.all_gather(appended, "mdl", axis=0, tiled=True)
    every_row = jnp.arange(seq_len, dtype=jnp.int32)
    suffix_ok = ((seg_row[None, :] == my_seg[:, None]) & (every_row[None, :] <= my_rows[:, None]))[
        :, None, None, :
    ]
    suffix_scores = (
        jnp.einsum(
            "rcgd,tcd->rcgt", q_rot, suffix[..., :head_dim], preferred_element_type=jnp.float32
        )
        * score_scale
    )
    suffix_scores = jnp.where(suffix_ok, suffix_scores, NEG)
    row_max = jnp.max(suffix_scores, -1)
    suffix_weights = jnp.where(suffix_ok, jnp.exp(suffix_scores - row_max[..., None]), 0.0)
    row_total = jnp.sum(suffix_weights, -1)
    mixed = jnp.einsum(
        "rcgt,tcd->rcgd",
        suffix_weights.astype(jnp.bfloat16),
        suffix[..., head_dim:],
        preferred_element_type=jnp.float32,
    )
    slot_ids = jnp.arange(slot_total, dtype=jnp.int32)
    pages_each = PREFIX // PAGE
    slot_prefix = jnp.sum(
        jnp.where(page_table[None, :] == slot_ids[:, None], (slot_ids // pages_each)[None, :], 0), 1
    )
    piece = lax.all_gather(prefix_cache, ("grp", "mdl"), axis=0, tiled=True)
    page_count = piece.shape[0]
    key_prefix = jnp.repeat(slot_prefix, page_len)
    allowed = (my_prefix[:, None] == key_prefix[None, :])[:, None, None, :]
    flat_pages = piece.reshape(page_count * page_len, kv_dev, 2 * head_dim)
    scores = (
        jnp.einsum(
            "rcgd,kcd->rcgk", q_rot, flat_pages[..., :head_dim], preferred_element_type=jnp.float32
        )
        * score_scale
    )
    scores = jnp.where(allowed, scores, NEG)
    new_max = jnp.maximum(row_max, jnp.max(scores, -1))
    factor = jnp.exp(row_max - new_max)
    page_weights = jnp.where(allowed, jnp.exp(scores - new_max[..., None]), 0.0)
    new_total = row_total * factor + jnp.sum(page_weights, -1)
    new_mixed = mixed * factor[..., None] + jnp.einsum(
        "rcgk,kcd->rcgd",
        page_weights.astype(jnp.bfloat16),
        flat_pages[..., head_dim:],
        preferred_element_type=jnp.float32,
    )
    attended = (
        (new_mixed / new_total[..., None])
        .astype(jnp.bfloat16)
        .reshape(rows_mdl, heads_dev * head_dim)
    )
    partial_out = jnp.dot(
        lax.all_gather(attended, "mdl", axis=0, tiled=True),
        w_out,
        preferred_element_type=jnp.float32,
    )
    residual = tokens + lax.psum_scatter(
        partial_out.astype(jnp.bfloat16), "tok", scatter_dimension=0, tiled=True
    ).astype(jnp.float32)
    squares_ffn = lax.psum(jnp.sum(residual * residual, -1), "mdl")
    ffn_input = (residual * lax.rsqrt(squares_ffn[:, None] / model_width + EPS) * ffn_gain).astype(
        jnp.bfloat16
    )
    w_pair = jnp.concatenate([w_gate, w_up], 1)
    ff_dev = w_gate.shape[1]
    partial_ffn = jnp.dot(
        lax.all_gather(ffn_input, "tok", axis=0, tiled=True),
        w_pair,
        preferred_element_type=jnp.float32,
    )
    summed = lax.psum_scatter(
        partial_ffn.astype(jnp.bfloat16), "mdl", scatter_dimension=0, tiled=True
    ).astype(jnp.float32)
    activated = (jax.nn.silu(summed[:, :ff_dev]) * summed[:, ff_dev:]).astype(jnp.bfloat16)
    partial_down = jnp.dot(
        lax.all_gather(activated, "mdl", axis=0, tiled=True),
        w_down,
        preferred_element_type=jnp.float32,
    )
    final_rows = residual + lax.psum_scatter(
        partial_down.astype(jnp.bfloat16), "tok", scatter_dimension=0, tiled=True
    ).astype(jnp.float32)
    tok_start = tok_idx * tok_rows
    my_tok_rows = tok_start + jnp.arange(tok_rows, dtype=jnp.int32)
    tok_seg = lax.dynamic_slice_in_dim(seg_row, tok_start, tok_rows)
    row_squares = jnp.sum(final_rows * final_rows, -1)
    req_squares = jnp.sum(
        jnp.where(tok_seg[:, None] == requests[None, :], row_squares[:, None], 0.0), 0
    )
    ends = offsets + counts - 1
    picked = ends[:, None] == my_tok_rows[None, :]
    last_part = jnp.sum(jnp.where(picked[:, :, None], final_rows[None, :, :], 0.0), 1)
    last_squares = jnp.sum(last_part * last_part, -1)
    packed = jnp.concatenate([last_part, req_squares[:, None], last_squares[:, None]], 1)
    packed = lax.psum(packed, "tok")
    blocks = lax.all_gather(packed, "mdl", axis=0, tiled=False)
    mdl_count = blocks.shape[0]
    last_rows = jnp.transpose(blocks[:, :, :feat_dev], (1, 0, 2)).reshape(req_count, model_width)
    req_total = jnp.sum(blocks[:, :, feat_dev], 0)
    last_total = jnp.sum(blocks[:, :, feat_dev + 1], 0)
    req_norm = jnp.sqrt(req_total / (counts.astype(jnp.float32) * model_width) + EPS)
    last_own = (last_rows * lax.rsqrt(last_total[:, None] / model_width + EPS) * final_gain).astype(
        jnp.bfloat16
    )
    last_normed = lax.all_gather(last_own, "grp", axis=0, tiled=True)
    logits = lax.dot_general(
        last_normed, lm_head, (((1,), (1,)), ((), ())), preferred_element_type=jnp.float32
    )
    local_max = jnp.max(logits, -1)
    local_max = lax.pmax(local_max, "mdl")
    local_max = lax.pmax(local_max, "tok")
    max_logit = lax.pmax(local_max, "grp").reshape(groups_total, req_count)
    return (
        final_rows.astype(jnp.bfloat16)[None],
        appended[None],
        req_norm[None],
        max_logit,
        logits,
    )


def solution(mesh):
    return jax.shard_map(
        on_device,
        mesh=mesh,
        in_specs=(
            P("grp", "tok", "mdl"),
            P(),
            P(),
            P(),
            P(("grp", "mdl"), None, "tok", None),
            P("mdl"),
            P("mdl", "tok"),
            P("mdl", "tok"),
            P("mdl", "tok"),
            P("tok", "mdl"),
            P("mdl"),
            P("mdl", "tok"),
            P("mdl", "tok"),
            P("tok", "mdl"),
            P(),
            P(("grp", "tok", "mdl"), None),
        ),
        out_specs=(
            P("grp", "tok", "mdl"),
            P("grp", "mdl", "tok", None),
            P("grp", None),
            P(),
            P(None, ("grp", "tok", "mdl")),
        ),
        check_vma=False,
    )
```

profile of v0, /device:TPU:32, one launch (start us, length us, event | category | flops | bytes accessed | tf_op | source)
XLA Modules:
  0.0 541.8 jit_solution(11023597313740727375)
XLA Ops:
  9.2 14.9 %psum.21 = f32[128]{0:T(128)S(1)} all-reduce(f32[128]{0:T(128)S(1)} %fusion.44), channel_id=1, replica_groups=mesh['grp'=4,'tok'=8,'mdl'=8] {'mdl'}, use_global_device_ids=true, to_apply=%region_1.0 | all-reduce | flops 128 | bytes 1024 | tf_op jit(solution)/shard_map/psum | solution.py:62
  24.1 1.7 fusion.46
  25.9 38.9 %all-gather.7.cloned.1.call-done = bf16[1024,640]{1,0:T(8,128)(2,1)} async-done(((bf16[128,640]{1,0:T(8,128)(2,1)}), bf16[1024,640]{1,0:T(8,128)(2,1)}) %all-gather.7.cloned.1.call-update) | async-done | bytes 1310736 | tf_op jit(solution)/shard_map/all_gather | solution.py:68
  64.7 5.1 fusion.30
  75.3 1.6 broadcast_compare_fusion
  76.9 32.9 %reduce-scatter.5.cloned.1.call-done = f32[128,896]{0,1:T(8,128)} async-done(((f32[1024,896]{0,1:T(8,128)}), f32[128,896]{0,1:T(8,128)}) %reduce-scatter.5.cloned.1.call-update) | async-done | bytes 458768 | tf_op jit(solution)/shard_map/reduce_scatter | solution.py:72
  112.6 1.9 copy.67
  116.4 13.2 %all_gather.28 = bf16[1024,1,256]{0,2,1:T(8,128)(2,1)} all-gather(bf16[128,1,256]{0,2,1:T(8,128)(2,1)S(1)} %get-tuple-element.25), channel_id=1, replica_groups=mesh['grp'=4,'tok'=8,'mdl'=8] {'mdl'}, dimensions={0}, use_global_device_ids=true | all-gather | bytes 589824 | tf_op jit(solution)/shard_map/all_gather | solution.py:97
  129.6 1.8 subtract_convert_fusion
  131.4 13.0 %fusion = (f32[128,5]{0,1:T(8,128)S(1)}, f32[128,5,8192]{2,0,1:T(8,128)}) fusion(pred[128,8192]{1,0:T(8,128)(4,1)} %broadcast_compare_fusion, bf16[8192,1,256]{2,0,1:T(8,128)(2,1)} %bitcast.163, bf16[128,5,64]{2,0,1:T(8,128)(2,1)} %get-tuple-element.19, bf16[128,5,64]{2,0,1:T(8,128)(2,1)} %get-tuple-element.18), kind=kOutput, calls=%fused_computation.2 | convolution fusion | flops 1358232960 | bytes 24447488 | tf_op jit(solution)/shard_map/rcgd,kcd->rcgk/dot_general | solution.py:129
  144.4 2.2 fusion.10
  146.6 14.2 %fusion.21 = f32[1,128,128,5]{2,1,3,0:T(8,128)} fusion(bf16[8192,1,256]{2,0,1:T(8,128)(2,1)} %bitcast.164, f32[128,5,8192]{2,0,1:T(8,128)} %get-tuple-element.35, f32[128,5]{0,1:T(8,128)S(1)} %max.23, pred[128,8192]{1,0:T(8,128)(4,1)} %broadcast_compare_fusion), kind=kOutput, calls=%fused_computation.28 | convolution fusion | flops 1368391680 | bytes 24447488 | tf_op jit(solution)/shard_map/rcgk,kcd->rcgd/dot_general | solution.py:139
  160.8 10.7 %fusion.1 = f32[128,5]{0,1:T(8,128)S(1)} fusion(f32[128,5,8192]{2,0,1:T(8,128)} %get-tuple-element.35, f32[128,5]{0,1:T(8,128)S(1)} %max.23, pred[128,8192]{1,0:T(8,128)(4,1)} %broadcast_compare_fusion), kind=kLoop, calls=%fused_computation.3 | loop fusion | flops 26213760 | bytes 22025216 | tf_op jit(solution)/shard_map/reduce_sum | solution.py:138
  172.6 1.5 fusion.39
  174.2 27.1 %all-gather.11.cloned.1.call-done = bf16[1024,640]{0,1:T(8,128)(2,1)} async-done(((bf16[128,640]{0,1:T(8,128)(2,1)}), bf16[1024,640]{0,1:T(8,128)(2,1)}) %all-gather.11.cloned.1.call-update) | async-done | bytes 1310736 | tf_op jit(solution)/shard_map/all_gather | solution.py:151
  201.3 4.0 convolution_convert_fusion.2
  205.4 40.1 %reduce-scatter.7.cloned.1.call-done = bf16[128,640]{1,0:T(8,128)(2,1)} async-done(((bf16[1024,640]{1,0:T(8,128)(2,1)}), bf16[128,640]{1,0:T(8,128)(2,1)}) %reduce-scatter.7.cloned.1.call-update) | async-done | bytes 163856 | tf_op jit(solution)/shard_map/reduce_scatter | solution.py:155
  246.5 12.4 %psum.22 = f32[128]{0:T(128)S(1)} all-reduce(f32[128]{0:T(128)S(1)} %multiply_reduce_fusion.1), channel_id=1, replica_groups=mesh['grp'=4,'tok'=8,'mdl'=8] {'mdl'}, use_global_device_ids=true, to_apply=%region_14.15 | all-reduce | flops 128 | bytes 1024 | tf_op jit(solution)/shard_map/psum | solution.py:158
  259.0 1.7 multiply_convert_fusion
  260.7 36.0 %all-gather.13.cloned.1.call-done = bf16[1024,640]{1,0:T(8,128)(2,1)} async-done(((bf16[128,640]{1,0:T(8,128)(2,1)}), bf16[1024,640]{1,0:T(8,128)(2,1)}) %all-gather.13.cloned.1.call-update) | async-done | bytes 1310736 | tf_op jit(solution)/shard_map/all_gather | solution.py:165
  296.7 10.5 %convolution_convert_fusion = bf16[1024,3584]{1,0:T(8,128)(2,1)} fusion(bf16[1024,640]{1,0:T(8,128)(2,1)} %all-gather.13.cloned.1.call-done, bf16[640,1792]{1,0:T(8,128)(2,1)} %param.28, bf16[640,1792]{1,0:T(8,128)(2,1)} %param.27), kind=kOutput, calls=%fused_computation.8 | convolution fusion | flops 4710465536 | bytes 13238272 | tf_op jit(solution)/shard_map/dot_general | solution.py:164
  307.3 49.0 %reduce-scatter.9.cloned.1.call-done = bf16[128,3584]{1,0:T(8,128)(2,1)} async-done(((bf16[1024,3584]{1,0:T(8,128)(2,1)}), bf16[128,3584]{1,0:T(8,128)(2,1)}) %reduce-scatter.9.cloned.1.call-update) | async-done | bytes 917520 | tf_op jit(solution)/shard_map/reduce_scatter | solution.py:169
  358.8 32.2 %all-gather.15.cloned.1.call-done = bf16[1024,1792]{1,0:T(8,128)(2,1)} async-done(((bf16[128,1792]{1,0:T(8,128)(2,1)}), bf16[1024,1792]{1,0:T(8,128)(2,1)}) %all-gather.15.cloned.1.call-update) | async-done | bytes 3670032 | tf_op jit(solution)/shard_map/all_gather | solution.py:174
  390.9 6.8 %convolution_convert_fusion.1 = bf16[1024,640]{1,0:T(8,128)(2,1)} fusion(bf16[1024,1792]{1,0:T(8,128)(2,1)} %all-gather.15.cloned.1.call-done, bf16[1792,640]{1,0:T(8,128)(2,1)} %param.29), kind=kOutput, calls=%fused_computation.21 | convolution fusion | flops 2349465600 | bytes 7274496 | tf_op jit(solution)/shard_map/dot_general | solution.py:173
  398.6 38.3 %reduce-scatter.11.cloned.1.call-done = bf16[128,640]{1,0:T(8,128)(2,1)} async-done(((bf16[1024,640]{1,0:T(8,128)(2,1)}), bf16[128,640]{1,0:T(8,128)(2,1)}) %reduce-scatter.11.cloned.1.call-update) | async-done | bytes 163856 | tf_op jit(solution)/shard_map/reduce_scatter | solution.py:178
  439.4 27.0 %psum.23 = f32[1,4,642]{2,1,0:T(4,128)S(1)} all-reduce(f32[1,4,642]{2,1,0:T(4,128)S(1)} %maximum_bitcast_fusion), channel_id=1, replica_groups=mesh['grp'=4,'tok'=8,'mdl'=8] {'tok'}, use_global_device_ids=true, to_apply=%region_21.22 | all-reduce | flops 2568 | bytes 20544 | tf_op jit(solution)/shard_map/psum | solution.py:193
  466.4 13.0 %all_gather.34 = f32[8,4,642]{2,1,0:T(4,128)S(1)} all-gather(f32[1,4,642]{2,1,0:T(4,128)S(1)} %psum.23), channel_id=1, replica_groups=mesh['grp'=4,'tok'=8,'mdl'=8] {'mdl'}, dimensions={0}, use_global_device_ids=true | all-gather | bytes 92448 | tf_op jit(solution)/shard_map/all_gather | solution.py:194
  480.2 12.3 %all-gather = bf16[4,4,5120]{2,1,0:T(4,128)(2,1)S(1)} all-gather(bf16[1,4,5120]{2,1,0:T(4,128)(2,1)S(1)} %fusion.52), channel_id=1, replica_groups=mesh['grp'=4,'tok'=8,'mdl'=8] {'grp'}, dimensions={0}, use_global_device_ids=true | all-gather | bytes 204800 | tf_op jit(solution)/shard_map/all_gather | solution.py:203
  492.6 1.6 fusion.70
  494.2 12.4 %pmax.21 = f32[16]{0:T(128)S(1)} all-reduce(f32[16]{0:T(128)S(1)} %get-tuple-element.36), channel_id=1, replica_groups=mesh['grp'=4,'tok'=8,'mdl'=8] {'mdl'}, use_global_device_ids=true, to_apply=%region_25.26 | all-reduce | flops 16 | bytes 128 | tf_op jit(solution)/shard_map/pmax | solution.py:208
  506.7 16.7 %pmax.22 = f32[16]{0:T(128)S(1)} all-reduce(f32[16]{0:T(128)S(1)} %pmax.21), channel_id=1, replica_groups=mesh['grp'=4,'tok'=8,'mdl'=8] {'tok'}, use_global_device_ids=true, to_apply=%region_26.27 | all-reduce | flops 16 | bytes 128 | tf_op jit(solution)/shard_map/pmax | solution.py:209
  523.5 10.8 %pmax.23 = f32[4,4]{1,0:T(4,128)} all-reduce(f32[4,4]{1,0:T(4,128)S(1)} %reshape.478), channel_id=1, replica_groups=mesh['grp'=4,'tok'=8,'mdl'=8] {'grp'}, use_global_device_ids=true, to_apply=%region_27.28 | all-reduce | flops 16 | bytes 128 | tf_op jit(solution)/shard_map/pmax | solution.py:210
  (95 shorter events, 20.4 us)
Async XLA Ops:
  8.0 484.6 %copy-start = (bf16[300,5120]{1,0:T(8,128)(2,1)S(1)}, bf16[300,5120]{1,0:T(8,128)(2,1)}, u32[]{:S(2)}) copy-start(bf16[300,5120]{1,0:T(8,128)(2,1)} %param.31) | copy-start | bytes 9216004
  8.0 56.7 %all-gather.7.cloned.1.call-start = ((), (), s32[]{:S(2)}) async-start(), calls=%async_computation.4 | async-start | bytes 1474560 | tf_op jit(solution)/shard_map/all_gather | solution.py:68
  25.8 84.0 %reduce-scatter.5.cloned.1.call-start = ((), (), s32[]{:S(2)}) async-start(), calls=%async_computation.5 | async-start | bytes 4128768 | tf_op jit(solution)/shard_map/reduce_scatter | solution.py:72
  69.9 0.7 copy-start.11
  69.9 61.5 %all-gather.9.cloned.1.call-start = ((), (), s32[]{:S(2)}) async-start(), calls=%async_computation.6 | async-start | bytes 4325376 | tf_op jit(solution)/shard_map/all_gather | solution.py:123
  70.5 130.9 %all-gather.11.cloned.1.call-start = ((), (), s32[]{:S(2)}) async-start(), calls=%async_computation.7 | async-start | bytes 1474560 | tf_op jit(solution)/shard_map/all_gather | solution.py:151
  131.4 13.0 %copy-start.4 = (bf16[1024,1,256]{0,2,1:T(8,128)(2,1)S(1)}, bf16[1024,1,256]{0,2,1:T(8,128)(2,1)}, u32[]{:S(2)}) copy-start(bf16[1024,1,256]{0,2,1:T(8,128)(2,1)} %all_gather.28) | copy-start | bytes 1572868
  131.4 13.0 %copy-start.6 = (pred[128,1024]{0,1:T(8,128)(4,1)S(1)}, pred[128,1024]{0,1:T(8,128)(4,1)}, u32[]{:S(2)}) copy-start(pred[128,1024]{0,1:T(8,128)(4,1)} %fusion.43) | copy-start | bytes 393220
  131.4 13.0 %copy-start.7 = (bf16[128,5,64]{2,0,1:T(8,128)(2,1)S(1)}, bf16[128,5,64]{2,0,1:T(8,128)(2,1)}, u32[]{:S(2)}) copy-start(bf16[128,5,64]{2,0,1:T(8,128)(2,1)} %get-tuple-element.18) | copy-start | bytes 245764
  131.4 13.0 %copy-start.8 = (bf16[128,5,64]{2,0,1:T(8,128)(2,1)S(1)}, bf16[128,5,64]{2,0,1:T(8,128)(2,1)}, u32[]{:S(2)}) copy-start(bf16[128,5,64]{2,0,1:T(8,128)(2,1)} %get-tuple-element.19) | copy-start | bytes 245764
  160.8 10.7 %copy-start.1 = (f32[1024,128,5]{1,0,2:T(8,128)S(1)}, f32[1024,128,5]{1,0,2:T(8,128)}, u32[]{:S(2)}) copy-start(f32[1024,128,5]{1,0,2:T(8,128)} %get-tuple-element.33) | copy-start | bytes 7864324
  171.5 1.0 copy-start.5
  171.5 1.1 copy-start.12
  174.1 71.4 %copy-start.2 = (bf16[1,128,640]{2,1,0:T(8,128)(2,1)S(1)}, bf16[1,128,640]{2,1,0:T(8,128)(2,1)}, u32[]{:S(2)}) copy-start(bf16[1,128,640]{2,1,0:T(8,128)(2,1)} %param.16) | copy-start | bytes 491524
  174.1 84.8 %copy-start.10 = (f32[640]{0:T(1024)S(1)}, f32[640]{0:T(1024)}, u32[]{:S(2)}) copy-start(f32[640]{0:T(1024)} %param.26) | copy-start | bytes 7684
  174.1 71.3 %reduce-scatter.7.cloned.1.call-start = ((), (), s32[]{:S(2)}) async-start(), calls=%async_computation.8 | async-start | bytes 1474560 | tf_op jit(solution)/shard_map/reduce_scatter | solution.py:155
  205.3 91.4 %all-gather.13.cloned.1.call-start = ((), (), s32[]{:S(2)}) async-start(), calls=%async_computation.9 | async-start | bytes 1474560 | tf_op jit(solution)/shard_map/all_gather | solution.py:165
  260.7 95.6 %reduce-scatter.9.cloned.1.call-start = ((), (), s32[]{:S(2)}) async-start(), calls=%async_computation.10 | async-start | bytes 8257536 | tf_op jit(solution)/shard_map/reduce_scatter | solution.py:169
  307.2 83.7 %all-gather.15.cloned.1.call-start = ((), (), s32[]{:S(2)}) async-start(), calls=%async_computation.11 | async-start | bytes 4128768 | tf_op jit(solution)/shard_map/all_gather | solution.py:174
  358.7 78.2 %copy-start.3 = (bf16[128,640]{1,0:T(8,128)(2,1)S(1)}, bf16[128,640]{1,0:T(8,128)(2,1)}, u32[]{:S(2)}) copy-start(bf16[128,640]{1,0:T(8,128)(2,1)} %reduce-scatter.7.cloned.1.call-done) | copy-start | bytes 491524
  358.7 78.2 %reduce-scatter.11.cloned.1.call-start = ((), (), s32[]{:S(2)}) async-start(), calls=%async_computation.12 | async-start | bytes 1474560 | tf_op jit(solution)/shard_map/reduce_scatter | solution.py:178
  397.8 82.3 %copy-start.9 = (f32[5120]{0:T(1024)S(1)}, f32[5120]{0:T(1024)}, u32[]{:S(2)}) copy-start(f32[5120]{0:T(1024)} %param.30) | copy-start | bytes 61444
Sparse Core Ops, SparseCore 0:
  26.0 38.7 all-gather.6
  70.0 39.7 reduce-scatter.4
  174.2 27.0 all-gather.10
  205.4 39.9 reduce-scatter.6
  260.8 35.8 all-gather.12
  307.3 48.8 reduce-scatter.8
  358.8 32.0 all-gather.14
  397.9 38.9 reduce-scatter.10
Sparse Core Ops, SparseCore 1:
  72.9 51.0 all-gather.8
where the time goes:
time: 543 us; the launch traced here: 542 us
  waiting for transfers between devices  295 us (54%)
  blocking collectives  133 us (24%)
  matrix products  58.8 us (11%)
  other arithmetic  28.5 us (5%)
  between operations  15.8 us (3%)
  local copies, waits for them, and re-layouts  10.3 us (2%)
    reduce_scatter x1, waiting for transfers between devices, on_device(): lax.psum_scatter(partial_ffn.astype(jnp.bfloat16), 'mdl', scatter_dimensi...  49 us
    reduce_scatter x1, waiting for transfers between devices, on_device(): lax.psum_scatter(partial_out.astype(jnp.bfloat16), 'tok', scatter_dimensi...  40.1 us
    all_gather x1, waiting for transfers between devices, on_device(): lax.all_gather(normed, 'tok', axis=0, tiled=True)  38.9 us
    reduce_scatter x1, waiting for transfers between devices, on_device(): lax.psum_scatter(partial_down.astype(jnp.bfloat16), 'tok', scatter_dimens...  38.3 us
    all_gather x1, waiting for transfers between devices, on_device(): lax.all_gather(ffn_input, 'tok', axis=0, tiled=True)  36 us
    reduce_scatter x1, waiting for transfers between devices, on_device(): lax.psum_scatter(partial_qkv, 'mdl', scatter_dimension=0, tiled=True)  32.9 us
    all_gather x1, waiting for transfers between devices, on_device(): lax.all_gather(activated, 'mdl', axis=0, tiled=True)  32.2 us
    all_gather x1, waiting for transfers between devices, on_device(): lax.all_gather(attended, 'mdl', axis=0, tiled=True)  27.1 us
  transfers between devices with their start and end apart: 9, of which 8 were waited for; matrix products, arithmetic and copies ran while one was open for 3% of the time, Pallas kernels for 0%

commit v1 on v0

--- a/solution.py
+++ b/solution.py
@@ -8,6 +8,12 @@
 EPS = 1e-06
 THETA = 1000000.0
 NEG = -1e30
+
+
+def unite_the_values(content):
+    a_name = "tok"
+    base_arr = jnp.concatenate([content] * lax.axis_size(a_name), axis=0)
+    return lax.all_to_all(base_arr, split_axis=0, tiled=True, axis_name=a_name, concat_axis=0)
 
 
 def rotate(tensor, positions):
@@ -161,11 +167,7 @@
     )
     w_pair = jnp.concatenate([w_gate, w_up], 1)
     ff_dev = w_gate.shape[1]
-    partial_ffn = jnp.dot(
-        lax.all_gather(ffn_input, "tok", axis=0, tiled=True),
-        w_pair,
-        preferred_element_type=jnp.float32,
-    )
+    partial_ffn = jnp.dot(unite_the_values(ffn_input), w_pair, preferred_element_type=jnp.float32)
     summed = lax.psum_scatter(
         partial_ffn.astype(jnp.bfloat16), "mdl", scatter_dimension=0, tiled=True
     ).astype(jnp.float32)

time: 543 us -> 538 us (level)
  waiting for transfers between devices: 295 us -> 255 us
  blocking collectives: 133 us -> 171 us
    all_to_all x0 -> x1, blocking collectives: none -> 38.5 us  [unite_the_values(): lax.all_to_all(base_arr, split_axis=0, tiled=True, axis_name=a_name, conc...]
    all_gather x1 -> x0, waiting for transfers between devices: 36 us -> none  [on_device(): lax.all_gather(ffn_input, 'tok', axis=0, tiled=True)]
  transfers between devices with their start and end apart: 9 -> 8, of which waited for: 8 -> 7; matrix products, arithmetic and copies ran while one was open for 3% -> 3% of each run, Pallas kernels for 0% -> 0%
where the time goes in v1:
time: 538 us; the launch traced here: 537 us
  waiting for transfers between devices  255 us (47%)
  blocking collectives  171 us (32%)
  matrix products  56.5 us (11%)
  other arithmetic  27.9 us (5%)
  between operations  15.9 us (3%)
  local copies, waits for them, and re-layouts  10.5 us (2%)
    reduce_scatter x1, waiting for transfers between devices, on_device(): lax.psum_scatter(partial_ffn.astype(jnp.bfloat16), 'mdl', scatter_dimensi...  44.9 us
    reduce_scatter x1, waiting for transfers between devices, on_device(): lax.psum_scatter(partial_out.astype(jnp.bfloat16), 'tok', scatter_dimensi...  40.1 us
    all_gather x1, waiting for transfers between devices, on_device(): lax.all_gather(normed, 'tok', axis=0, tiled=True)  38.9 us
    all_to_all x1, blocking collectives, unite_the_values(): lax.all_to_all(base_arr, split_axis=0, tiled=True, axis_name=a_name, conc...  38.5 us
    reduce_scatter x1, waiting for transfers between devices, on_device(): lax.psum_scatter(partial_down.astype(jnp.bfloat16), 'tok', scatter_dimens...  38.3 us
    reduce_scatter x1, waiting for transfers between devices, on_device(): lax.psum_scatter(partial_qkv, 'mdl', scatter_dimension=0, tiled=True)  32.9 us
    all_gather x1, waiting for transfers between devices, on_device(): lax.all_gather(activated, 'mdl', axis=0, tiled=True)  32.2 us
    all_gather x1, waiting for transfers between devices, on_device(): lax.all_gather(attended, 'mdl', axis=0, tiled=True)  27.1 us
  transfers between devices with their start and end apart: 8, of which 7 were waited for; matrix products, arithmetic and copies ran while one was open for 3% of the time, Pallas kernels for 0%

profile of v1, /device:TPU:32, one launch (start us, length us, event | category | flops | bytes accessed | tf_op | source)
XLA Modules:
  0.0 537.2 jit_solution(7645066216428883610)
XLA Ops:
  9.2 14.9 %psum.21 = f32[128]{0:T(128)S(1)} all-reduce(f32[128]{0:T(128)S(1)} %fusion.44), channel_id=1, replica_groups=mesh['grp'=4,'tok'=8,'mdl'=8] {'mdl'}, use_global_device_ids=true, to_apply=%region_1.0 | all-reduce | flops 128 | bytes 1024 | tf_op jit(solution)/shard_map/psum | solution.py:68
  24.1 1.7 fusion.46
  25.9 38.9 %all-gather.6.cloned.1.call-done = bf16[1024,640]{1,0:T(8,128)(2,1)} async-done(((bf16[128,640]{1,0:T(8,128)(2,1)}), bf16[1024,640]{1,0:T(8,128)(2,1)}) %all-gather.6.cloned.1.call-update) | async-done | bytes 1310736 | tf_op jit(solution)/shard_map/all_gather | solution.py:74
  64.7 5.1 fusion.30
  75.3 1.6 broadcast_compare_fusion
  76.9 32.9 %reduce-scatter.5.cloned.1.call-done = f32[128,896]{0,1:T(8,128)} async-done(((f32[1024,896]{0,1:T(8,128)}), f32[128,896]{0,1:T(8,128)}) %reduce-scatter.5.cloned.1.call-update) | async-done | bytes 458768 | tf_op jit(solution)/shard_map/reduce_scatter | solution.py:78
  112.6 1.9 copy.67
  116.4 13.2 %all_gather.25 = bf16[1024,1,256]{0,2,1:T(8,128)(2,1)} all-gather(bf16[128,1,256]{0,2,1:T(8,128)(2,1)S(1)} %get-tuple-element.27), channel_id=1, replica_groups=mesh['grp'=4,'tok'=8,'mdl'=8] {'mdl'}, dimensions={0}, use_global_device_ids=true | all-gather | bytes 589824 | tf_op jit(solution)/shard_map/all_gather | solution.py:103
  129.6 1.8 subtract_convert_fusion
  131.4 13.0 %fusion = (f32[128,5]{0,1:T(8,128)S(1)}, f32[128,5,8192]{2,0,1:T(8,128)}) fusion(pred[128,8192]{1,0:T(8,128)(4,1)} %broadcast_compare_fusion, bf16[8192,1,256]{2,0,1:T(8,128)(2,1)} %bitcast.168, bf16[128,5,64]{2,0,1:T(8,128)(2,1)} %get-tuple-element.21, bf16[128,5,64]{2,0,1:T(8,128)(2,1)} %get-tuple-element.20), kind=kOutput, calls=%fused_computation.2 | convolution fusion | flops 1358232960 | bytes 24447488 | tf_op jit(solution)/shard_map/rcgd,kcd->rcgk/dot_general | solution.py:135
  144.4 2.2 fusion.10
  146.6 14.2 %fusion.21 = f32[1,128,128,5]{2,1,3,0:T(8,128)} fusion(bf16[8192,1,256]{2,0,1:T(8,128)(2,1)} %bitcast.169, f32[128,5,8192]{2,0,1:T(8,128)} %get-tuple-element.37, f32[128,5]{0,1:T(8,128)S(1)} %max.23, pred[128,8192]{1,0:T(8,128)(4,1)} %broadcast_compare_fusion), kind=kOutput, calls=%fused_computation.28 | convolution fusion | flops 1368391680 | bytes 24447488 | tf_op jit(solution)/shard_map/rcgk,kcd->rcgd/dot_general | solution.py:145
  160.8 10.7 %fusion.1 = f32[128,5]{0,1:T(8,128)S(1)} fusion(f32[128,5,8192]{2,0,1:T(8,128)} %get-tuple-element.37, f32[128,5]{0,1:T(8,128)S(1)} %max.23, pred[128,8192]{1,0:T(8,128)(4,1)} %broadcast_compare_fusion), kind=kLoop, calls=%fused_computation.3 | loop fusion | flops 26213760 | bytes 22025216 | tf_op jit(solution)/shard_map/reduce_sum | solution.py:144
  172.6 1.5 fusion.39
  174.2 27.1 %all-gather.10.cloned.1.call-done = bf16[1024,640]{0,1:T(8,128)(2,1)} async-done(((bf16[128,640]{0,1:T(8,128)(2,1)}), bf16[1024,640]{0,1:T(8,128)(2,1)}) %all-gather.10.cloned.1.call-update) | async-done | bytes 1310736 | tf_op jit(solution)/shard_map/all_gather | solution.py:157
  201.3 4.0 convolution_convert_fusion.2
  205.4 40.1 %reduce-scatter.7.cloned.1.call-done = bf16[128,640]{1,0:T(8,128)(2,1)} async-done(((bf16[1024,640]{1,0:T(8,128)(2,1)}), bf16[128,640]{1,0:T(8,128)(2,1)}) %reduce-scatter.7.cloned.1.call-update) | async-done | bytes 163856 | tf_op jit(solution)/shard_map/reduce_scatter | solution.py:161
  246.5 12.4 %psum.22 = f32[128]{0:T(128)S(1)} all-reduce(f32[128]{0:T(128)S(1)} %multiply_reduce_fusion.1), channel_id=1, replica_groups=mesh['grp'=4,'tok'=8,'mdl'=8] {'mdl'}, use_global_device_ids=true, to_apply=%region_14.15 | all-reduce | flops 128 | bytes 1024 | tf_op jit(solution)/shard_map/psum | solution.py:164
  260.2 38.5 %all_to_all.12 = bf16[8,128,640]{2,1,0:T(8,128)(2,1)S(1)} all-to-all(bf16[8,128,640]{2,1,0:T(8,128)(2,1)S(1)} %bitcast.157), channel_id=1, replica_groups=mesh['grp'=4,'tok'=8,'mdl'=8] {'tok'}, dimensions={0} | all-to-all | bytes 2621440 | tf_op jit(solution)/shard_map/all_to_all | solution.py:16
  298.7 8.1 %convolution_convert_fusion = bf16[1024,3584]{1,0:T(8,128)(2,1)} fusion(bf16[1024,640]{1,0:T(8,128)(2,1)S(1)} %bitcast.158, bf16[640,1792]{1,0:T(8,128)(2,1)S(1)} %copy-done.11, bf16[640,1792]{1,0:T(8,128)(2,1)S(1)} %copy-done.12), kind=kOutput, calls=%fused_computation.8 | convolution fusion | flops 4710465536 | bytes 13238272 | tf_op jit(solution)/shard_map/dot_general | solution.py:170
  306.9 44.9 %reduce-scatter.9.cloned.1.call-done = bf16[128,3584]{1,0:T(8,128)(2,1)} async-done(((bf16[1024,3584]{1,0:T(8,128)(2,1)}), bf16[128,3584]{1,0:T(8,128)(2,1)}) %reduce-scatter.9.cloned.1.call-update) | async-done | bytes 917520 | tf_op jit(solution)/shard_map/reduce_scatter | solution.py:171
  351.8 1.4 convert_element_type.104
  354.3 32.2 %all-gather.12.cloned.1.call-done = bf16[1024,1792]{1,0:T(8,128)(2,1)} async-done(((bf16[128,1792]{1,0:T(8,128)(2,1)}), bf16[1024,1792]{1,0:T(8,128)(2,1)}) %all-gather.12.cloned.1.call-update) | async-done | bytes 3670032 | tf_op jit(solution)/shard_map/all_gather | solution.py:176
  386.4 6.8 %convolution_convert_fusion.1 = bf16[1024,640]{1,0:T(8,128)(2,1)} fusion(bf16[1024,1792]{1,0:T(8,128)(2,1)} %all-gather.12.cloned.1.call-done, bf16[1792,640]{1,0:T(8,128)(2,1)} %param.29), kind=kOutput, calls=%fused_computation.21 | convolution fusion | flops 2349465600 | bytes 7274496 | tf_op jit(solution)/shard_map/dot_general | solution.py:175
  394.1 38.3 %reduce-scatter.11.cloned.1.call-done = bf16[128,640]{1,0:T(8,128)(2,1)} async-done(((bf16[1024,640]{1,0:T(8,128)(2,1)}), bf16[128,640]{1,0:T(8,128)(2,1)}) %reduce-scatter.11.cloned.1.call-update) | async-done | bytes 163856 | tf_op jit(solution)/shard_map/reduce_scatter | solution.py:180
  434.8 27.0 %psum.23 = f32[1,4,642]{2,1,0:T(4,128)S(1)} all-reduce(f32[1,4,642]{2,1,0:T(4,128)S(1)} %maximum_bitcast_fusion), channel_id=1, replica_groups=mesh['grp'=4,'tok'=8,'mdl'=8] {'tok'}, use_global_device_ids=true, to_apply=%region_21.22 | all-reduce | flops 2568 | bytes 20544 | tf_op jit(solution)/shard_map/psum | solution.py:195
  461.8 13.0 %all_gather.30 = f32[8,4,642]{2,1,0:T(4,128)S(1)} all-gather(f32[1,4,642]{2,1,0:T(4,128)S(1)} %psum.23), channel_id=1, replica_groups=mesh['grp'=4,'tok'=8,'mdl'=8] {'mdl'}, dimensions={0}, use_global_device_ids=true | all-gather | bytes 92448 | tf_op jit(solution)/shard_map/all_gather | solution.py:196
  475.7 12.3 %all-gather = bf16[4,4,5120]{2,1,0:T(4,128)(2,1)S(1)} all-gather(bf16[1,4,5120]{2,1,0:T(4,128)(2,1)S(1)} %fusion.52), channel_id=1, replica_groups=mesh['grp'=4,'tok'=8,'mdl'=8] {'grp'}, dimensions={0}, use_global_device_ids=true | all-gather | bytes 204800 | tf_op jit(solution)/shard_map/all_gather | solution.py:205
  488.1 1.6 fusion.70
  489.8 12.4 %pmax.21 = f32[16]{0:T(128)S(1)} all-reduce(f32[16]{0:T(128)S(1)} %get-tuple-element.38), channel_id=1, replica_groups=mesh['grp'=4,'tok'=8,'mdl'=8] {'mdl'}, use_global_device_ids=true, to_apply=%region_25.26 | all-reduce | flops 16 | bytes 128 | tf_op jit(solution)/shard_map/pmax | solution.py:210
  502.2 16.7 %pmax.22 = f32[16]{0:T(128)S(1)} all-reduce(f32[16]{0:T(128)S(1)} %pmax.21), channel_id=1, replica_groups=mesh['grp'=4,'tok'=8,'mdl'=8] {'tok'}, use_global_device_ids=true, to_apply=%region_26.27 | all-reduce | flops 16 | bytes 128 | tf_op jit(solution)/shard_map/pmax | solution.py:211
  519.0 10.8 %pmax.23 = f32[4,4]{1,0:T(4,128)} all-reduce(f32[4,4]{1,0:T(4,128)S(1)} %reshape.480), channel_id=1, replica_groups=mesh['grp'=4,'tok'=8,'mdl'=8] {'grp'}, use_global_device_ids=true, to_apply=%region_27.28 | all-reduce | flops 16 | bytes 128 | tf_op jit(solution)/shard_map/pmax | solution.py:212
  (104 shorter events, 20.2 us)
Async XLA Ops:
  8.0 480.1 %copy-start = (bf16[300,5120]{1,0:T(8,128)(2,1)S(1)}, bf16[300,5120]{1,0:T(8,128)(2,1)}, u32[]{:S(2)}) copy-start(bf16[300,5120]{1,0:T(8,128)(2,1)} %param.31) | copy-start | bytes 9216004
  8.0 56.7 %all-gather.6.cloned.1.call-start = ((), (), s32[]{:S(2)}) async-start(), calls=%async_computation.5 | async-start | bytes 1474560 | tf_op jit(solution)/shard_map/all_gather | solution.py:74
  25.8 84.0 %reduce-scatter.5.cloned.1.call-start = ((), (), s32[]{:S(2)}) async-start(), calls=%async_computation.6 | async-start | bytes 4128768 | tf_op jit(solution)/shard_map/reduce_scatter | solution.py:78
  69.9 0.7 copy-start.13
  69.9 61.5 %all-gather.8.cloned.1.call-start = ((), (), s32[]{:S(2)}) async-start(), calls=%async_computation.7 | async-start | bytes 4325376 | tf_op jit(solution)/shard_map/all_gather | solution.py:129
  70.5 130.9 %all-gather.10.cloned.1.call-start = ((), (), s32[]{:S(2)}) async-start(), calls=%async_computation.8 | async-start | bytes 1474560 | tf_op jit(solution)/shard_map/all_gather | solution.py:157
  131.4 13.0 %copy-start.4 = (bf16[1024,1,256]{0,2,1:T(8,128)(2,1)S(1)}, bf16[1024,1,256]{0,2,1:T(8,128)(2,1)}, u32[]{:S(2)}) copy-start(bf16[1024,1,256]{0,2,1:T(8,128)(2,1)} %all_gather.25) | copy-start | bytes 1572868
  131.4 13.0 %copy-start.6 = (pred[128,1024]{0,1:T(8,128)(4,1)S(1)}, pred[128,1024]{0,1:T(8,128)(4,1)}, u32[]{:S(2)}) copy-start(pred[128,1024]{0,1:T(8,128)(4,1)} %fusion.43) | copy-start | bytes 393220
  131.4 13.0 %copy-start.7 = (bf16[128,5,64]{2,0,1:T(8,128)(2,1)S(1)}, bf16[128,5,64]{2,0,1:T(8,128)(2,1)}, u32[]{:S(2)}) copy-start(bf16[128,5,64]{2,0,1:T(8,128)(2,1)} %get-tuple-element.20) | copy-start | bytes 245764
  131.4 13.0 %copy-start.8 = (bf16[128,5,64]{2,0,1:T(8,128)(2,1)S(1)}, bf16[128,5,64]{2,0,1:T(8,128)(2,1)}, u32[]{:S(2)}) copy-start(bf16[128,5,64]{2,0,1:T(8,128)(2,1)} %get-tuple-element.21) | copy-start | bytes 245764
  160.8 10.7 %copy-start.1 = (f32[1024,128,5]{1,0,2:T(8,128)S(1)}, f32[1024,128,5]{1,0,2:T(8,128)}, u32[]{:S(2)}) copy-start(f32[1024,128,5]{1,0,2:T(8,128)} %get-tuple-element.35) | copy-start | bytes 7864324
  171.5 1.0 copy-start.5
  171.5 1.1 copy-start.14
  174.1 71.4 %copy-start.2 = (bf16[1,128,640]{2,1,0:T(8,128)(2,1)S(1)}, bf16[1,128,640]{2,1,0:T(8,128)(2,1)}, u32[]{:S(2)}) copy-start(bf16[1,128,640]{2,1,0:T(8,128)(2,1)} %param.16) | copy-start | bytes 491524
  174.1 84.8 %copy-start.10 = (f32[640]{0:T(1024)S(1)}, f32[640]{0:T(1024)}, u32[]{:S(2)}) copy-start(f32[640]{0:T(1024)} %param.26) | copy-start | bytes 7684
  174.1 71.3 %reduce-scatter.7.cloned.1.call-start = ((), (), s32[]{:S(2)}) async-start(), calls=%async_computation.9 | async-start | bytes 1474560 | tf_op jit(solution)/shard_map/reduce_scatter | solution.py:161
  205.3 146.5 %reduce-scatter.9.cloned.1.call-start = ((), (), s32[]{:S(2)}) async-start(), calls=%async_computation.10 | async-start | bytes 8257536 | tf_op jit(solution)/shard_map/reduce_scatter | solution.py:171
  260.0 38.7 %copy-start.11 = (bf16[640,1792]{1,0:T(8,128)(2,1)S(1)}, bf16[640,1792]{1,0:T(8,128)(2,1)}, u32[]{:S(2)}) copy-start(bf16[640,1792]{1,0:T(8,128)(2,1)} %param.28) | copy-start | bytes 6881284
  260.0 38.7 %copy-start.12 = (bf16[640,1792]{1,0:T(8,128)(2,1)S(1)}, bf16[640,1792]{1,0:T(8,128)(2,1)}, u32[]{:S(2)}) copy-start(bf16[640,1792]{1,0:T(8,128)(2,1)} %param.27) | copy-start | bytes 6881284
  306.8 79.6 %all-gather.12.cloned.1.call-start = ((), (), s32[]{:S(2)}) async-start(), calls=%async_computation.11 | async-start | bytes 4128768 | tf_op jit(solution)/shard_map/all_gather | solution.py:176
  354.2 78.2 %copy-start.3 = (bf16[128,640]{1,0:T(8,128)(2,1)S(1)}, bf16[128,640]{1,0:T(8,128)(2,1)}, u32[]{:S(2)}) copy-start(bf16[128,640]{1,0:T(8,128)(2,1)} %reduce-scatter.7.cloned.1.call-done) | copy-start | bytes 491524
  354.2 78.2 %reduce-scatter.11.cloned.1.call-start = ((), (), s32[]{:S(2)}) async-start(), calls=%async_computation.12 | async-start | bytes 1474560 | tf_op jit(solution)/shard_map/reduce_scatter | solution.py:180
  393.3 82.4 %copy-start.9 = (f32[5120]{0:T(1024)S(1)}, f32[5120]{0:T(1024)}, u32[]{:S(2)}) copy-start(f32[5120]{0:T(1024)} %param.30) | copy-start | bytes 61444
Sparse Core Ops, SparseCore 0:
  26.0 38.7 all-gather.5
  70.0 39.7 reduce-scatter.4
  174.2 27.0 all-gather.9
  205.4 39.9 reduce-scatter.6
  307.0 44.7 reduce-scatter.8
  354.3 32.0 all-gather.11
  393.4 38.9 reduce-scatter.10
Sparse Core Ops, SparseCore 1:
  72.9 51.0 all-gather.7
